TPU v7x, 32 devices: a whole 2x2x4 slice. The times are simulated.
32 devices in a mesh: chain: 8 (over z, x), grp: 4 (over y, core).
Axes of the slice: x: 2, y: 2, z: 4, core: 2. Of those that a mesh axis runs over, the one named last changes fastest.
Arguments:
- right_side: float32 [16, 4, 64, 128], P('chain', 'grp'), may hold values from -0.8 to 0.8
- factor: float32 [16, 4, 2, 128, 128], P('chain', 'grp'), may hold values from -1 to 1
- inverse_diag: float32 [16, 4, 128, 128], P('chain', 'grp'), as said below
- pattern: int32 [16, 4, 2], P('chain'), may hold values from 0 to 3, as said below
Outputs:
- forward_result: float32 [16, 4, 64, 128], P('chain', 'grp')
- solution: float32 [16, 4, 64, 128], P('chain', 'grp')
Inputs may be any that keep to these rules, and one draw needn't show every extreme that they name: `pattern`: the 2 entries of one supernode are different supernodes of the previous level. `inverse_diag`: every block is lower triangular with a diagonal between 0.75 and 1.05.
All inputs are finite; a program needn't handle non-finite values.
Results may differ from a plain program's by a relative error of at most 0.0002.
Values sent between devices are 32-bit elements; how exact they have to be, the bound alone decides.
No kernel may reach another device: no remote copies, remote signals or barrier semaphores. Data moves between devices by JAX's collectives and lax.ppermute only.
A program may use at most 320 MiB of HBM per device.

v0:
```python
import jax
import jax.numpy as jnp
from jax import lax
from jax.sharding import PartitionSpec as P

PRECISE = lax.Precision.HIGHEST


def carried_in(value, axis, join, neutral, backward):
    count, mine = (lax.axis_size(axis), lax.axis_index(axis))
    pieces = jax.tree.map(lambda part: lax.all_gather(part, axis), value)
    if backward:
        pieces = jax.tree.map(lambda part: part[::-1], pieces)
        mine = count - 1 - mine
    subtotal = jax.tree.map(
        lambda part, zero: jnp.full_like(part, 0) + jnp.asarray(zero, part.dtype), value, neutral
    )

    def hop(position, subtotal):
        longer = join(subtotal, jax.tree.map(lambda part: part[position], pieces))
        return jax.tree.map(lambda new, old: jnp.where(position < mine, new, old), longer, subtotal)

    return lax.fori_loop(0, count - 1, hop, subtotal)


def matmul(left_side, right_factor):
    return jnp.dot(left_side, right_factor, precision=PRECISE, preferred_element_type=jnp.float32)


def matmul_trans(left_side, right_factor):
    return lax.dot_general(
        left_side,
        right_factor,
        (((1,), (1,)), ((), ())),
        precision=PRECISE,
        preferred_element_type=jnp.float32,
    )


def combine_forward(earlier_map, later_map):
    return (
        matmul(earlier_map[0], later_map[0]),
        matmul(earlier_map[1], later_map[0]) + later_map[1],
    )


def combine_backward(earlier_map, later_map):
    return (
        matmul(later_map[0], earlier_map[0]),
        matmul_trans(earlier_map[1], later_map[0]) + later_map[1],
    )


def fold_maps(running, inputs):
    return ((matmul(running[0], inputs[0]), matmul(running[1], inputs[0]) + inputs[1]), None)


def forward_step(previous, inputs):
    updated = matmul(previous, inputs[0]) + inputs[1]
    return (updated, updated)


def back_fold(running, inputs):
    return (matmul_trans(running - inputs[1], inputs[0]), None)


def shards(right_side, factor, inverse_diag, pattern):
    levels = right_side.shape[0]
    samples = right_side.shape[2]
    sup_rows = right_side.shape[3]
    groups = lax.axis_size("grp")
    level_rows = groups * sup_rows
    my_group = lax.axis_index("grp")
    scaled = jnp.einsum(
        "lgti,lgkij->lgktj",
        inverse_diag,
        factor,
        precision=PRECISE,
        preferred_element_type=jnp.float32,
    )
    lifted = jnp.einsum(
        "lgsi,lgti->lgst",
        right_side,
        inverse_diag,
        precision=PRECISE,
        preferred_element_type=jnp.float32,
    )
    blocks, offsets = (
        lax.all_gather(scaled, "grp", axis=1, tiled=True),
        lax.all_gather(lifted, "grp", axis=1, tiled=True),
    )
    onehot = (pattern[..., None] == jnp.arange(groups, dtype=jnp.int32)).astype(jnp.float32)
    level_maps = -jnp.einsum(
        "lgkh,lgktj->lhjgt", onehot, blocks, precision=PRECISE, preferred_element_type=jnp.float32
    )
    level_maps = level_maps.reshape(levels, level_rows, level_rows)
    sources = offsets.transpose(0, 2, 1, 3).reshape(levels, samples, level_rows)
    (total_map, total_shift), _ = lax.scan(
        fold_maps, (level_maps[0], sources[0]), (level_maps[1:], sources[1:])
    )
    neutral = (
        jnp.eye(level_rows, dtype=jnp.float32),
        jnp.zeros((samples, level_rows), jnp.float32),
    )
    _, incoming = carried_in((total_map, total_shift), "chain", combine_forward, neutral, False)
    _, solved = lax.scan(forward_step, incoming, (level_maps, sources))
    forward_own = lax.dynamic_slice_in_dim(solved, my_group * sup_rows, sup_rows, 2)
    back_shift, _ = lax.scan(
        back_fold, jnp.zeros((samples, level_rows), jnp.float32), (level_maps, solved), reverse=True
    )
    _, arriving = carried_in((total_map, back_shift), "chain", combine_backward, neutral, True)
    own_inverse = inverse_diag[:, 0]

    def back_step(running, inputs):
        level_map, forward_rows, inverse = inputs
        own_rows = lax.dynamic_slice_in_dim(forward_rows, my_group * sup_rows, sup_rows, 1)
        own_pending = lax.dynamic_slice_in_dim(running, my_group * sup_rows, sup_rows, 1)
        answer = matmul(own_rows - own_pending, inverse)
        return (matmul_trans(running - forward_rows, level_map), answer)

    _, answers = lax.scan(back_step, arriving, (level_maps, solved, own_inverse), reverse=True)
    return (forward_own[:, None], answers[:, None])


def solution(mesh):
    return jax.shard_map(
        shards,
        mesh=mesh,
        in_specs=(
            P("chain", "grp", None, None),
            P("chain", "grp", None, None, None),
            P("chain", "grp", None, None),
            P("chain", None, None),
        ),
        out_specs=(P("chain", "grp", None, None), P("chain", "grp", None, None)),
        check_vma=False,
    )
```

profile of v0, /device:TPU:0, one launch (start us, length us, event | category | flops | bytes accessed | tf_op | source)
XLA Modules:
  0.0 289.6 jit_solution(16148861564298682824)
XLA Ops:
  7.2 0.9 copy-done
  8.1 1.5 convolution_bitcast_fusion.4
  9.6 0.8 copy.22
  10.5 0.8 copy.23
  11.3 1.3 fusion.50
  12.6 7.2 %all-gather.1 = f32[2,256,128]{2,1,0:T(8,128)S(1)} all-gather(f32[2,64,128]{2,1,0:T(8,128)S(1)} %fusion.50), channel_id=3, replica_groups=mesh['chain'=8,'grp'=4] {'grp'}, dimensions={1}, use_global_device_ids=true | all-gather | bytes 327680 | tf_op jit(solution)/shard_map/all_gather | solution.py:90
  20.0 0.7 fusion.58
  20.8 9.2 %all-gather.9.cloned.1.call-done = f32[2,4,2,128,128]{4,3,2,0,1:T(8,128)} async-done(((f32[2,1,2,128,128]{4,3,2,0,1:T(8,128)}), f32[2,4,2,128,128]{4,3,2,0,1:T(8,128)}) %all-gather.9.cloned.1.call-update) | async-done | bytes 1048592 | tf_op jit(solution)/shard_map/all_gather | solution.py:89
  30.1 3.9 %negate_bitcast_fusion = f32[2,4,128,4,128]{2,1,4,3,0:T(4,128)S(1)} fusion(f32[2,4,2,128,128]{4,3,2,0,1:T(8,128)} %all-gather.9.cloned.1.call-done, s32[2,4,2]{2,1,0:T(4,128)S(1)} %copy.23), kind=kOutput, calls=%fused_computation.46 | convolution fusion | flops 13107264 | bytes 3145792 | tf_op jit(solution)/shard_map/lgkh,lgktj->lhjgt/dot_general | solution.py:93
  34.0 1.1 fusion.57
  35.1 1.8 convolution_add_fusion
  37.0 5.7 %fusion.39 = f32[512,512]{1,0:T(8,128)} fusion(f32[64,8,4,128]{3,2,1,0:T(4,128)} %bitcast.155, f32[64,8,4,128]{3,2,1,0:T(4,128)S(1)} %bitcast.154), kind=kOutput, calls=%fused_computation.50 | convolution fusion | flops 1610612736 | bytes 3145728 | tf_op jit(solution)/shard_map/while/body/eval_jaxpr/dot_general | solution.py:27
  42.9 1.1 reshape.43
  44.0 1.9 reshape.42
  45.9 1.9 copy.26
  47.8 29.5 %all-gather.13.cloned.1.call-done = f32[512,512]{1,0:T(8,128)} async-done(((f32[64,512]{1,0:T(8,128)}), f32[512,512]{1,0:T(8,128)}) %all-gather.13.cloned.1.call-update) | async-done | bytes 1048592 | tf_op jit(solution)/shard_map/all_gather | solution.py:11
  77.3 125.4 %all-gather.11.cloned.1.call-done = f32[4096,512]{1,0:T(8,128)} async-done(((f32[512,512]{1,0:T(8,128)}), f32[4096,512]{1,0:T(8,128)}) %all-gather.11.cloned.1.call-update) | async-done | bytes 8388624 | tf_op jit(solution)/shard_map/all_gather | solution.py:11
  202.7 14.4 %while.79 = (s32[]{:T(128)}, f32[64,512]{1,0:T(8,128)S(1)}, s32[]{:T(128)}, f32[8,512,512]{2,1,0:T(8,128)}, f32[8,64,512]{2,1,0:T(8,128)}, /*index=5*/s32[]{:T(128)}, s32[]{:T(128)}) while((s32[]{:T(128)}, f32[64,512]{1,0:T(8,128)S(1)}, s32[]{:T(128)}, f32[8,512,512]{2,1,0:T(8,128)}, f32[8,64,512]{2,1,0:T(8,128)}, ...), condition=%wide.region_1.2_spmd.clone, body=%wide.region_0.1_spmd.clone.sunk | while | flops 201457664 | bytes 1837671 | solution.py:23
  202.7 2.0 fusion.82
  204.8 2.0 fusion.82
  206.8 2.0 fusion.82
  208.9 2.0 fusion.82
  211.0 2.0 fusion.82
  213.0 2.0 fusion.82
  215.1 2.0 fusion.82
  217.1 1.7 while.76
  217.1 0.8 bitcast_dynamic-update-slice_fusion.2
  218.0 0.8 bitcast_dynamic-update-slice_fusion.2
  218.8 2.3 while.77
  218.8 1.1 fusion.75
  220.0 1.1 fusion.75
  221.1 0.6 copy-done.1
  221.8 7.6 %rev.6 = f32[8,512,512]{2,1,0:T(8,128)} reverse(f32[8,512,512]{2,1,0:T(8,128)} %get-tuple-element.945), dimensions={0} | reverse | bytes 16777216 | tf_op jit(solution)/shard_map/rev | solution.py:13
  229.4 0.6 dynamic-slice_bitcast_fusion
  230.0 30.4 %all-gather.15.cloned.1.call-done = f32[512,512]{1,0:T(8,128)} async-done(((f32[64,512]{1,0:T(8,128)}), f32[512,512]{1,0:T(8,128)}) %all-gather.15.cloned.1.call-update) | async-done | bytes 1048592 | tf_op jit(solution)/shard_map/all_gather | solution.py:11
  260.4 2.3 rev.7
  262.7 16.8 %while.80 = (s32[]{:T(128)}, f32[64,512]{1,0:T(8,128)S(1)}, s32[]{:T(128)}, f32[8,512,512]{2,1,0:T(8,128)}, f32[8,64,512]{2,1,0:T(8,128)}, /*index=5*/s32[]{:T(128)}, s32[]{:T(128)}) while((s32[]{:T(128)}, f32[64,512]{1,0:T(8,128)S(1)}, s32[]{:T(128)}, f32[8,512,512]{2,1,0:T(8,128)}, f32[8,64,512]{2,1,0:T(8,128)}, ...), condition=%wide.region_7.8_spmd.clone, body=%wide.region_6.7_spmd.clone.sunk | while | flops 201457664 | bytes 1837671 | solution.py:23
  262.7 2.4 fusion.85
  265.2 2.4 fusion.85
  267.6 2.4 fusion.85
  270.0 2.4 fusion.85
  272.4 2.4 fusion.85
  274.8 2.4 fusion.85
  277.2 2.4 fusion.85
  279.6 2.8 while.78
  279.9 1.1 fusion.78
  281.3 1.1 fusion.78
  282.4 0.6 copy-done.5
  (45 shorter events, 1.4 us)
Async XLA Ops:
  7.2 1.0 copy-start
  7.2 22.9 %all-gather.9.cloned.1.call-start = ((), (), s32[]{:S(2)}) async-start(), calls=%async_computation | async-start | bytes 1310720 | tf_op jit(solution)/shard_map/all_gather | solution.py:89
  10.5 66.9 %all-gather.13.cloned.1.call-start = ((), (), s32[]{:S(2)}) async-start(), calls=%async_computation.2 | async-start | bytes 1179648 | tf_op jit(solution)/shard_map/all_gather | solution.py:11
  20.0 0.8 copy-start.3
  34.0 1.2 copy-start.4
  36.9 165.8 %all-gather.11.cloned.1.call-start = ((), (), s32[]{:S(2)}) async-start(), calls=%async_computation.1 | async-start | bytes 9437184 | tf_op jit(solution)/shard_map/all_gather | solution.py:11
  42.7 217.7 %all-gather.15.cloned.1.call-start = ((), (), s32[]{:S(2)}) async-start(), calls=%async_computation.3 | async-start | bytes 1179648 | tf_op jit(solution)/shard_map/all_gather | solution.py:11
  221.1 0.6 copy-start.1
  262.7 16.9 %copy-start.2 = (f32[2,1,128,128]{3,2,1,0:T(8,128)S(1)}, f32[2,1,128,128]{3,2,1,0:T(8,128)}, u32[]{:S(2)}) copy-start(f32[2,1,128,128]{3,2,1,0:T(8,128)} %param.16) | copy-start | bytes 393220
  282.4 0.6 copy-start.5
Sparse Core Ops, SparseCore 0:
  10.6 19.4 all-gather.8
  37.0 40.2 all-gather.12
  79.5 123.1 all-gather.10
  221.9 38.4 all-gather.14
where the time goes:
time: 290 us
  waiting for transfers between devices  195 us (67%)
  matrix products  51.5 us (18%)
  local copies, waits for them, and re-layouts  21.4 us (7%)
  between operations  13.9 us (5%)
  blocking collectives  7.25 us (2%)
    all_gather x3, waiting for transfers between devices, carried_in(): pieces = jax.tree.map(lambda part: lax.all_gather(part, axis), value)  185 us
    dot_general x13, matrix products, matmul(): jnp.dot(left_side, right_factor, precision=PRECISE, preferred_element_typ...  23.7 us
    dot_general x11, matrix products, matmul_trans(): lax.dot_general(left_side, right_factor, (((1,), (1,)), ((), ())), precis...  21 us
    rev x2, local copies, waits for them, and re-layouts, carried_in(): pieces = jax.tree.map(lambda part: part[::-1], pieces)  9.88 us
    all_gather x1, waiting for transfers between devices, shards(): lax.all_gather(scaled, 'grp', axis=1, tiled=True)  9.25 us
    all_gather x1, blocking collectives, shards(): lax.all_gather(lifted, 'grp', axis=1, tiled=True)  7.25 us
  transfers between devices with their start and end apart: 4, of which 4 were waited for; matrix products, arithmetic and copies ran while one was open for 8% of the time, Pallas kernels for 0%

commit v1 on v0

--- a/solution.py
+++ b/solution.py
@@ -4,6 +4,22 @@
 from jax.sharding import PartitionSpec as P
 
 PRECISE = lax.Precision.HIGHEST
+
+
+def gather_around(x, axis, dim):
+    ways, here, turn = (lax.axis_size(axis), lax.axis_index(axis), x.shape[dim])
+    shape = [n * ways if d == dim else n for d, n in enumerate(x.shape)]
+    full = lax.dynamic_update_slice_in_dim(jnp.zeros(shape, x.dtype), x, here * turn, axis=dim)
+    going_up = going_down = x
+    for far in range(1, ways // 2 + 1):
+        going_up = lax.ppermute(going_up, axis, [(d, (d + 1) % ways) for d in range(ways)])
+        full = lax.dynamic_update_slice_in_dim(full, going_up, (here - far) % ways * turn, axis=dim)
+        if 2 * far < ways:
+            going_down = lax.ppermute(going_down, axis, [(d, (d - 1) % ways) for d in range(ways)])
+            full = lax.dynamic_update_slice_in_dim(
+                full, going_down, (here + far) % ways * turn, axis=dim
+            )
+    return full
 
 
 def carried_in(value, axis, join, neutral, backward):
@@ -87,7 +103,7 @@
     )
     blocks, offsets = (
         lax.all_gather(scaled, "grp", axis=1, tiled=True),
-        lax.all_gather(lifted, "grp", axis=1, tiled=True),
+        gather_around(lifted, "grp", 1),
     )
     onehot = (pattern[..., None] == jnp.arange(groups, dtype=jnp.int32)).astype(jnp.float32)
     level_maps = -jnp.einsum(

time: 290 us -> 290 us (level)
  blocking collectives: 7.25 us -> 0 us
  local copies, waits for them, and re-layouts: 21.4 us -> 26.7 us
  starting transfers between devices: 0.34 us -> 3.45 us
    all_gather x1 -> x0, blocking collectives: 7.25 us -> none  [shards(): lax.all_gather(lifted, 'grp', axis=1, tiled=True)]
    dynamic_update_slice x0 -> x4, local copies, waits for them, and re-layouts: none -> 5.39 us  [the longest x2 2.7 us: gather_around(): lax.dynamic_update_slice_in_dim(full, going_up, (here - far) % ways * tur...]
    ppermute x0 -> x3, starting transfers between devices: none -> 3.11 us  [the longest x1 2.01 us: gather_around(): lax.ppermute(going_down, axis, [(d, (d - 1) % ways) for d in range(ways)])]
    all_gather x1, waiting for transfers between devices: 9.25 us -> 6.21 us  [shards(): lax.all_gather(scaled, 'grp', axis=1, tiled=True)]
  transfers between devices with their start and end apart: 4 -> 7, of which waited for: 4 -> 5; matrix products, arithmetic and copies ran while one was open for 8% -> 9% of each run, Pallas kernels for 0% -> 0%
where the time goes in v1:
time: 290 us
  waiting for transfers between devices  193 us (67%)
  matrix products  51.5 us (18%)
  local copies, waits for them, and re-layouts  26.7 us (9%)
  between operations  14 us (5%)
  starting transfers between devices  3.45 us (1%)
    all_gather x3, waiting for transfers between devices, carried_in(): pieces = jax.tree.map(lambda part: lax.all_gather(part, axis), value)  185 us
    dot_general x13, matrix products, matmul(): jnp.dot(left_side, right_factor, precision=PRECISE, preferred_element_typ...  23.7 us
    dot_general x11, matrix products, matmul_trans(): lax.dot_general(left_side, right_factor, (((1,), (1,)), ((), ())), precis...  21 us
    rev x2, local copies, waits for them, and re-layouts, carried_in(): pieces = jax.tree.map(lambda part: part[::-1], pieces)  9.88 us
    all_gather x1, waiting for transfers between devices, shards(): lax.all_gather(scaled, 'grp', axis=1, tiled=True)  6.21 us
  transfers between devices with their start and end apart: 7, of which 5 were waited for; matrix products, arithmetic and copies ran while one was open for 9% of the time, Pallas kernels for 0%

profile of v1, /device:TPU:0, one launch (start us, length us, event | category | flops | bytes accessed | tf_op | source)
XLA Modules:
  0.0 289.6 jit_solution(15318879153333158815)
XLA Ops:
  7.2 0.9 copy-done
  8.1 1.5 convolution_bitcast_fusion.4
  9.6 0.8 copy.28
  10.5 1.3 fusion.50
  12.4 2.0 collective-permute-start.1
  14.4 1.9 collective-permute-done
  17.6 1.3 dynamic_update_slice.27
  19.0 1.3 dynamic_update_slice.28
  20.4 1.3 dynamic_update_slice.29
  21.7 1.3 dynamic_update_slice.30
  23.9 6.2 %all-gather.8.cloned.1.call-done = f32[2,4,2,128,128]{4,3,2,0,1:T(8,128)} async-done(((f32[2,1,2,128,128]{4,3,2,0,1:T(8,128)}), f32[2,4,2,128,128]{4,3,2,0,1:T(8,128)}) %all-gather.8.cloned.1.call-update) | async-done | bytes 1048592 | tf_op jit(solution)/shard_map/all_gather | solution.py:105
  30.1 3.9 %negate_bitcast_fusion = f32[2,4,128,4,128]{2,1,4,3,0:T(4,128)S(1)} fusion(f32[2,4,2,128,128]{4,3,2,0,1:T(8,128)} %all-gather.8.cloned.1.call-done, s32[2,4,2]{2,1,0:T(4,128)S(1)} %copy.29), kind=kOutput, calls=%fused_computation.46 | convolution fusion | flops 13107264 | bytes 3145792 | tf_op jit(solution)/shard_map/lgkh,lgktj->lhjgt/dot_general | solution.py:109
  34.0 1.2 fusion.57
  35.1 1.8 convolution_add_fusion
  37.0 5.7 %fusion.39 = f32[512,512]{1,0:T(8,128)} fusion(f32[64,8,4,128]{3,2,1,0:T(4,128)} %bitcast.158, f32[64,8,4,128]{3,2,1,0:T(4,128)S(1)} %bitcast.157), kind=kOutput, calls=%fused_computation.50 | convolution fusion | flops 1610612736 | bytes 3145728 | tf_op jit(solution)/shard_map/while/body/eval_jaxpr/dot_general | solution.py:43
  43.0 1.1 reshape.43
  44.0 1.9 reshape.42
  45.9 1.9 copy.35
  47.8 29.5 %all-gather.12.cloned.1.call-done = f32[512,512]{1,0:T(8,128)} async-done(((f32[64,512]{1,0:T(8,128)}), f32[512,512]{1,0:T(8,128)}) %all-gather.12.cloned.1.call-update) | async-done | bytes 1048592 | tf_op jit(solution)/shard_map/all_gather | solution.py:27
  77.4 125.4 %all-gather.10.cloned.1.call-done = f32[4096,512]{1,0:T(8,128)} async-done(((f32[512,512]{1,0:T(8,128)}), f32[4096,512]{1,0:T(8,128)}) %all-gather.10.cloned.1.call-update) | async-done | bytes 8388624 | tf_op jit(solution)/shard_map/all_gather | solution.py:27
  202.7 14.4 %while.79 = (s32[]{:T(128)}, f32[64,512]{1,0:T(8,128)S(1)}, s32[]{:T(128)}, f32[8,512,512]{2,1,0:T(8,128)}, f32[8,64,512]{2,1,0:T(8,128)}, /*index=5*/s32[]{:T(128)}, s32[]{:T(128)}) while((s32[]{:T(128)}, f32[64,512]{1,0:T(8,128)S(1)}, s32[]{:T(128)}, f32[8,512,512]{2,1,0:T(8,128)}, f32[8,64,512]{2,1,0:T(8,128)}, ...), condition=%wide.region_1.2_spmd.clone, body=%wide.region_0.1_spmd.clone.sunk | while | flops 201457664 | bytes 1837671 | solution.py:39
  202.7 2.0 fusion.82
  204.8 2.0 fusion.82
  206.9 2.0 fusion.82
  208.9 2.0 fusion.82
  211.0 2.0 fusion.82
  213.1 2.0 fusion.82
  215.1 2.0 fusion.82
  217.1 1.7 while.76
  217.2 0.8 bitcast_dynamic-update-slice_fusion.2
  218.0 0.8 bitcast_dynamic-update-slice_fusion.2
  218.8 2.3 while.77
  218.9 1.1 fusion.75
  220.0 1.1 fusion.75
  221.8 7.6 %rev.6 = f32[8,512,512]{2,1,0:T(8,128)} reverse(f32[8,512,512]{2,1,0:T(8,128)} %get-tuple-element.945), dimensions={0} | reverse | bytes 16777216 | tf_op jit(solution)/shard_map/rev | solution.py:29
  230.1 30.4 %all-gather.14.cloned.1.call-done = f32[512,512]{1,0:T(8,128)} async-done(((f32[64,512]{1,0:T(8,128)}), f32[512,512]{1,0:T(8,128)}) %all-gather.14.cloned.1.call-update) | async-done | bytes 1048592 | tf_op jit(solution)/shard_map/all_gather | solution.py:27
  260.4 2.3 rev.7
  262.7 16.8 %while.80 = (s32[]{:T(128)}, f32[64,512]{1,0:T(8,128)S(1)}, s32[]{:T(128)}, f32[8,512,512]{2,1,0:T(8,128)}, f32[8,64,512]{2,1,0:T(8,128)}, /*index=5*/s32[]{:T(128)}, s32[]{:T(128)}) while((s32[]{:T(128)}, f32[64,512]{1,0:T(8,128)S(1)}, s32[]{:T(128)}, f32[8,512,512]{2,1,0:T(8,128)}, f32[8,64,512]{2,1,0:T(8,128)}, ...), condition=%wide.region_7.8_spmd.clone, body=%wide.region_6.7_spmd.clone.sunk | while | flops 201457664 | bytes 1837671 | solution.py:39
  262.8 2.4 fusion.85
  265.2 2.4 fusion.85
  267.6 2.4 fusion.85
  270.0 2.4 fusion.85
  272.4 2.4 fusion.85
  274.8 2.4 fusion.85
  277.2 2.4 fusion.85
  279.6 2.8 while.78
  279.9 1.1 fusion.78
  281.3 1.1 fusion.78
  (54 shorter events, 5.7 us)
Async XLA Ops:
  7.2 1.0 copy-start
  7.2 22.9 %all-gather.8.cloned.1.call-start = ((), (), s32[]{:S(2)}) async-start(), calls=%async_computation | async-start | bytes 1310720 | tf_op jit(solution)/shard_map/all_gather | solution.py:105
  10.5 66.9 %all-gather.12.cloned.1.call-start = ((), (), s32[]{:S(2)}) async-start(), calls=%async_computation.2 | async-start | bytes 1179648 | tf_op jit(solution)/shard_map/all_gather | solution.py:27
  11.8 4.4 %collective-permute-start = (f32[2,1,64,128]{3,2,0,1:T(8,128)S(1)}, f32[2,1,64,128]{3,2,0,1:T(8,128)S(1)}, u32[]{:S(2)}, u32[]{:S(2)}) collective-permute-start(f32[2,1,64,128]{3,2,0,1:T(8,128)S(1)} %bitcast.166), channel_id=1, source_target_pairs={{0,1},{1,2},{2,3},{3,0},{4,5},{5,6},{6,7},{7,4},{8,9},{9,10},{10,1... | collective-permute-start | bytes 196616 | tf_op jit(solution)/shard_map/ppermute | solution.py:15
  12.4 8.0 %collective-permute-start.1 = (f32[2,1,64,128]{3,2,0,1:T(8,128)S(1)}, f32[2,1,64,128]{3,2,0,1:T(8,128)S(1)}, u32[]{:S(2)}, u32[]{:S(2)}) collective-permute-start(f32[2,1,64,128]{3,2,0,1:T(8,128)S(1)} %bitcast.167), channel_id=1, source_target_pairs={{0,3},{1,0},{2,1},{3,2},{4,7},{5,4},{6,5},{7,6},{8,11},{9,8},{10,9... | collective-permute-start | bytes 196616 | tf_op jit(solution)/shard_map/ppermute | solution.py:18
  16.3 5.5 %collective-permute-start.2 = (f32[2,1,64,128]{3,2,0,1:T(8,128)S(1)}, f32[2,1,64,128]{3,2,0,1:T(8,128)S(1)}, u32[]{:S(2)}, u32[]{:S(2)}) collective-permute-start(f32[2,1,64,128]{3,2,0,1:T(8,128)S(1)} %collective-permute-done), channel_id=1, source_target_pairs={{0,1},{1,2},{2,3},{3,0},{4,5},{5,6},{6,7},{7,4},{8,9},{9,10},{10,1... | collective-permute-start | bytes 196616 | tf_op jit(solution)/shard_map/ppermute | solution.py:15
  23.1 0.8 copy-start.3
  34.0 1.2 copy-start.4
  37.0 165.8 %all-gather.10.cloned.1.call-start = ((), (), s32[]{:S(2)}) async-start(), calls=%async_computation.1 | async-start | bytes 9437184 | tf_op jit(solution)/shard_map/all_gather | solution.py:27
  42.7 217.7 %all-gather.14.cloned.1.call-start = ((), (), s32[]{:S(2)}) async-start(), calls=%async_computation.3 | async-start | bytes 1179648 | tf_op jit(solution)/shard_map/all_gather | solution.py:27
  221.1 0.6 copy-start.1
  262.7 16.9 %copy-start.2 = (f32[2,1,128,128]{3,2,1,0:T(8,128)S(1)}, f32[2,1,128,128]{3,2,1,0:T(8,128)}, u32[]{:S(2)}) copy-start(f32[2,1,128,128]{3,2,1,0:T(8,128)} %param.16) | copy-start | bytes 393220
  282.4 0.6 copy-start.5
Sparse Core Ops, SparseCore 0:
  10.6 19.4 all-gather.7
  37.1 40.2 all-gather.11
  79.5 123.1 all-gather.9
  221.9 38.4 all-gather.13
